TPU v7x, 32 devices: a whole 2x2x4 slice. The times are simulated.
32 devices in a mesh: vis: 8 (over y, x, core), tile: 4 (over z).
Axes of the slice: x: 2, y: 2, z: 4, core: 2. Of those that a mesh axis runs over, the one named last changes fastest.
Arguments:
- image: float32 [8192, 8192], P('vis', 'tile'), may hold values from 0 to 2
- extrapolated: float32 [8192, 8192], P('vis', 'tile'), may hold values from -6 to 6
- vis_dual: float32 [8192, 2, 128], P(('vis', 'tile')), may hold values from -6 to 6
- tree_dual: float32 [2, 8192, 4096], P(None, 'vis', 'tile'), may hold values from -6 to 6
- observed: float32 [8192, 2, 128], P(('vis', 'tile')), may hold values from -6 to 6
- kernel: float32 [128, 128], replicated, may hold values from -0.5 to 0.5
- block_index: int32 [8192], P(('vis', 'tile')), may hold values from 0 to 16383
- live_blocks: int32 [32], P(('vis', 'tile')), may hold values from 1 to 256, as said below
Outputs:
- image_next: float32 [8192, 8192], P('vis', 'tile')
- vis_next: float32 [8192, 2, 128], P(('vis', 'tile'))
- tree_next: float32 [2, 8192, 4096], P(None, 'vis', 'tile')
Inputs may be any that keep to these rules, and one draw needn't show every extreme that they name: Each device's live slots are its first live_blocks entries of 256; some device has all 256 live in every draw.
All inputs are finite; a program needn't handle non-finite values.
Results may differ from a plain program's by a relative error of at most 0.00005.
Values sent between devices are 32-bit elements; how exact they have to be, the bound alone decides.
No kernel may reach another device: no remote copies, remote signals or barrier semaphores. Data moves between devices by JAX's collectives and lax.ppermute only.
A program may use at most 192 MiB of HBM per device.

v0:
```python
import math
import jax
import jax.numpy as jnp
from jax import lax
from jax.sharding import PartitionSpec as P

LOW_TAPS = (
    -0.010597401784997278,
    0.032883011666982945,
    0.030841381835986965,
    -0.18703481171888114,
    -0.02798376941698385,
    0.6308807679295904,
    0.7148465705525415,
    0.23037781330885523,
)
HIGH_TAPS = tuple(
    ((1.0 if position % 2 == 0 else -1.0) * LOW_TAPS[7 - position] for position in range(8))
)
TWO_PI = 2.0 * math.pi


def shifted(block, axis, distance):
    devices = range(lax.axis_size(axis))
    route = [((i - distance) % len(devices), i) for i in devices]
    return lax.ppermute(block, axis, route)


def phase_table(left_ids, right_ids, period):
    turns = left_ids[:, None] * right_ids[None, :] % period
    angles = turns.astype(jnp.float32) * (TWO_PI / period)
    return (jnp.cos(angles), jnp.sin(angles))


def factor_pair(length):
    chosen_factor = 1
    for candidate in range(1, math.isqrt(length) + 1):
        if length % candidate == 0:
            chosen_factor = candidate
    return (chosen_factor, length // chosen_factor)


def complex_einsum(form, left_real, left_imag, table_cos, table_sin, real_only):
    precise = lax.Precision.HIGHEST
    real_part = jnp.einsum(form, left_real, table_cos, precision=precise)
    if left_imag is not None:
        real_part = real_part - jnp.einsum(form, left_imag, table_sin, precision=precise)
    if real_only:
        return (real_part, None)
    imag_part = jnp.einsum(form, left_real, table_sin, precision=precise)
    if left_imag is not None:
        imag_part = imag_part + jnp.einsum(form, left_imag, table_cos, precision=precise)
    return (imag_part * 0.0 + real_part, imag_part)


def transform_axis(real_in, imag_in, sign_value, along, real_only):
    length = real_in.shape[along]
    first_factor, second_factor = factor_pair(length)
    first_ids = jnp.arange(first_factor, dtype=jnp.int32)
    second_ids = jnp.arange(second_factor, dtype=jnp.int32)
    cos_first, sin_first = phase_table(first_ids, first_ids, first_factor)
    cos_twist, sin_twist = phase_table(first_ids, second_ids, length)
    cos_second, sin_second = phase_table(second_ids, second_ids, second_factor)
    sin_twist = sign_value * sin_twist
    if along == 0:
        other_len = real_in.shape[1]
        shape_in = (first_factor, second_factor, other_len)
        form_first = "abm,ca->cbm"
        form_second = "cbm,db->dcm"
        cos_twist = cos_twist[:, :, None]
        sin_twist = sin_twist[:, :, None]
        shape_out = (length, other_len)
    else:
        other_len = real_in.shape[0]
        shape_in = (other_len, first_factor, second_factor)
        form_first = "mab,ca->mcb"
        form_second = "mcb,db->mdc"
        cos_twist = cos_twist[None, :, :]
        sin_twist = sin_twist[None, :, :]
        shape_out = (other_len, length)
    shaped_real = real_in.reshape(shape_in)
    shaped_imag = None if imag_in is None else imag_in.reshape(shape_in)
    section_real, section_imag = complex_einsum(
        form_first, shaped_real, shaped_imag, cos_first, sign_value * sin_first, False
    )
    twisted_real = section_real * cos_twist - section_imag * sin_twist
    twisted_imag = section_real * sin_twist + section_imag * cos_twist
    out_real, out_imag = complex_einsum(
        form_second, twisted_real, twisted_imag, cos_second, sign_value * sin_second, real_only
    )
    if real_only:
        return (out_real.reshape(shape_out), None)
    return (out_real.reshape(shape_out), out_imag.reshape(shape_out))


def analyse_local(coarse):
    half_rows = coarse.shape[1] // 2
    next_rows = shifted(coarse[:, :6], "tile", -1)
    extended = jnp.concatenate([coarse, next_rows], axis=1)
    phases = [lax.slice_in_dim(extended, parity, extended.shape[1], 2, 1) for parity in range(2)]
    approx = jnp.zeros((coarse.shape[0], half_rows), jnp.float32)
    detail = jnp.zeros_like(approx)
    for position in range(8):
        strided = lax.slice_in_dim(
            phases[position % 2], position // 2, position // 2 + half_rows, 1, 1
        )
        approx = approx + LOW_TAPS[position] * strided
        detail = detail + HIGH_TAPS[position] * strided
    return (approx, detail)


def upsample(ext_approx, ext_detail):
    out_rows = ext_detail.shape[1] - 3
    even_part = jnp.zeros((ext_detail.shape[0], out_rows), jnp.float32)
    odd_part = jnp.zeros_like(even_part)
    for lag_index in range(4):
        window_detail = ext_detail[:, 3 - lag_index : 3 - lag_index + out_rows]
        even_part = even_part + HIGH_TAPS[2 * lag_index] * window_detail
        odd_part = odd_part + HIGH_TAPS[2 * lag_index + 1] * window_detail
        if ext_approx is not None:
            window_approx = ext_approx[:, 3 - lag_index : 3 - lag_index + out_rows]
            even_part = even_part + LOW_TAPS[2 * lag_index] * window_approx
            odd_part = odd_part + LOW_TAPS[2 * lag_index + 1] * window_approx
    return jnp.stack([even_part, odd_part], axis=2).reshape(ext_detail.shape[0], 2 * out_rows)


def split_three(values):
    first = lax.reduce_precision(values, exponent_bits=8, mantissa_bits=7)
    rest = values - first
    second = lax.reduce_precision(rest, exponent_bits=8, mantissa_bits=7)
    third = rest - second
    pieces = [first, second, third]
    return jnp.concatenate([piece.astype(jnp.bfloat16) for piece in pieces], axis=-1)


def pick_rows(index, table):
    width = table.shape[1]
    selector = (index[:, None] == jnp.arange(table.shape[0], dtype=jnp.int32)[None, :]).astype(
        jnp.bfloat16
    )
    summed = jnp.dot(selector, split_three(table), preferred_element_type=jnp.float32)
    return summed[:, :width] + summed[:, width : 2 * width] + summed[:, 2 * width :]


def rows_to_grid(local_rows, values, row_count):
    groups, members, width = values.shape
    pieces = split_three(values)
    selector = (
        jnp.arange(row_count, dtype=jnp.int32)[None, :, None] == local_rows[:, None, :]
    ).astype(jnp.bfloat16)
    summed = jnp.einsum("gkb,gbc->gkc", selector, pieces, preferred_element_type=jnp.float32)
    summed = summed[..., :width] + summed[..., width : 2 * width] + summed[..., 2 * width :]
    return summed.reshape(groups * row_count, width)


def on_device(image, extrapolated, vis_dual, tree_dual, observed, kernel, block_index, live_blocks):
    precise = lax.Precision.HIGHEST
    slab_rows, slab_cols = image.shape
    n_vis = lax.axis_size("vis")
    n_tile = lax.axis_size("tile")
    vis_id = lax.axis_index("vis")
    tile_id = lax.axis_index("tile")
    len_rows = slab_rows * n_vis
    len_cols = slab_cols * n_tile
    block_width = kernel.shape[0]
    chunk = slab_cols // n_vis
    slot_count = vis_dual.shape[0]
    norm_scale = 1.0 / math.sqrt(len_rows * len_cols)
    columns = lax.all_to_all(extrapolated, "vis", split_axis=1, concat_axis=0, tiled=True)
    spec_real, spec_imag = transform_axis(columns, None, -1.0, 0, False)
    all_index = lax.all_gather(block_index, ("vis", "tile"), tiled=True)
    total_blocks = all_index.shape[0]
    owner = jnp.arange(total_blocks, dtype=jnp.int32) // slot_count
    per_row = slab_cols // block_width
    local_row = all_index // per_row
    row_of = owner // n_tile * slab_rows + local_row
    band_of = owner % n_tile * per_row + all_index % per_row
    col_ids = tile_id * slab_cols + vis_id * chunk + jnp.arange(chunk, dtype=jnp.int32)
    band_count = len_cols // block_width
    band_turns = (
        (jnp.arange(band_count, dtype=jnp.int32) * block_width)[:, None]
        * col_ids[None, :]
        % len_cols
    )
    band_angles = band_turns.astype(jnp.float32) * (TWO_PI / len_cols)
    band_both = pick_rows(band_of, jnp.concatenate([jnp.cos(band_angles), jnp.sin(band_angles)], 1))
    band_cos = band_both[:, :chunk]
    band_sin = band_both[:, chunk:]
    cell_turns = col_ids[:, None] * jnp.arange(block_width, dtype=jnp.int32)[None, :] % len_cols
    cell_angles = cell_turns.astype(jnp.float32) * (TWO_PI / len_cols)
    cell_cos = jnp.cos(cell_angles)
    cell_sin = jnp.sin(cell_angles)
    picked_real = jnp.take(spec_real, row_of, axis=0)
    picked_imag = jnp.take(spec_imag, row_of, axis=0)
    twisted_real = picked_real * band_cos + picked_imag * band_sin
    twisted_imag = picked_imag * band_cos - picked_real * band_sin
    part_real = jnp.dot(twisted_real, cell_cos, precision=precise) + jnp.dot(
        twisted_imag, cell_sin, precision=precise
    )
    part_imag = jnp.dot(twisted_imag, cell_cos, precision=precise) - jnp.dot(
        twisted_real, cell_sin, precision=precise
    )
    partial = jnp.stack([part_real, part_imag], axis=1)
    partial = lax.all_to_all(partial, "vis", split_axis=0, concat_axis=0, tiled=True)
    partial = partial.reshape((n_vis, total_blocks // n_vis) + partial.shape[1:]).sum(axis=0)
    partial = lax.all_to_all(partial, "tile", split_axis=0, concat_axis=0, tiled=True)
    chosen = partial.reshape((n_tile, slot_count) + partial.shape[1:]).sum(axis=0) * norm_scale
    model = jnp.einsum("ij,csj->csi", kernel, chosen, precision=precise)
    live_mask = (jnp.arange(slot_count, dtype=jnp.int32) < live_blocks[0]).astype(jnp.float32)[
        :, None, None
    ]
    misfit = (vis_dual / 0.5 + model - observed) * live_mask
    totals = lax.psum((jnp.sum(misfit * misfit), jnp.sum(live_mask)), ("vis", "tile"))
    radius = jnp.sqrt(2.0 * block_width * totals[1])
    size_now = jnp.sqrt(totals[0])
    vis_next = 0.5 * misfit * (1.0 - radius / jnp.maximum(size_now, radius))
    contrib = jnp.einsum("ij,csi->csj", kernel, vis_next, precision=precise)
    every = lax.all_gather(contrib, "tile", tiled=True)
    every = lax.all_gather(every, "vis", tiled=True)
    back_real = jnp.dot(every[:, 0, :], cell_cos.T, precision=precise) - jnp.dot(
        every[:, 1, :], cell_sin.T, precision=precise
    )
    back_imag = jnp.dot(every[:, 0, :], cell_sin.T, precision=precise) + jnp.dot(
        every[:, 1, :], cell_cos.T, precision=precise
    )
    turned_real = back_real * band_cos - back_imag * band_sin
    turned_imag = back_real * band_sin + back_imag * band_cos
    turned = jnp.concatenate([turned_real, turned_imag], axis=1)
    turned = turned.reshape(n_vis, total_blocks // n_vis, 2 * chunk)
    gridded = rows_to_grid(local_row.reshape(n_vis, total_blocks // n_vis), turned, slab_rows)
    pixel_real, unused_part = transform_axis(gridded[:, :chunk], gridded[:, chunk:], 1.0, 0, True)
    data_term = (
        lax.all_to_all(pixel_real, "vis", split_axis=0, concat_axis=1, tiled=True) * norm_scale
    )
    approx_one, detail_one = analyse_local(extrapolated)
    approx_two, detail_two = analyse_local(approx_one)
    child = tree_dual[0] + 0.5 * detail_one
    parent = tree_dual[1] + 0.5 * jnp.repeat(detail_two, 2, axis=1)
    factor = 1.0 / jnp.maximum(jnp.sqrt(child * child + parent * parent), 1.0)
    child_next = child * factor
    parent_next = parent * factor
    parent_sum = parent_next[:, 0::2] + parent_next[:, 1::2]
    parent_tail = shifted(parent_sum[:, -3:], "tile", 1)
    level_one = upsample(None, jnp.concatenate([parent_tail, parent_sum], axis=1))
    both_tails = shifted(jnp.stack([level_one[:, -3:], child_next[:, -3:]]), "tile", 1)
    prior_term = upsample(
        jnp.concatenate([both_tails[0], level_one], axis=1),
        jnp.concatenate([both_tails[1], child_next], axis=1),
    )
    image_next = jnp.maximum(image - 0.5 * (data_term + prior_term), 0.0)
    return (image_next, vis_next, jnp.stack([child_next, parent_next]))


def solution(mesh):
    return jax.shard_map(
        on_device,
        mesh=mesh,
        in_specs=(
            P("vis", "tile"),
            P("vis", "tile"),
            P(("vis", "tile"), None, None),
            P(None, "vis", "tile"),
            P(("vis", "tile"), None, None),
            P(),
            P(("vis", "tile")),
            P(("vis", "tile")),
        ),
        out_specs=(P("vis", "tile"), P(("vis", "tile"), None, None), P(None, "vis", "tile")),
        check_vma=False,
    )
```

profile of v0, /device:TPU:0, one launch (start us, length us, event | category | flops | bytes accessed | tf_op | source)
XLA Modules:
  0.0 1235.9 jit_solution(12371021110578368048)
XLA Ops:
  7.2 9.3 copy.239
  21.8 70.9 %all-gather = s32[32,1,256]{2,1,0:T(1,128)S(1)} all-gather(s32[1,1,256]{2,1,0:T(1,128)S(1)} %bitcast.146), channel_id=1, replica_groups=mesh['vis'=8,'tile'=4] {'vis','tile'}, dimensions={0}, use_global_device_ids=true | all-gather | bytes 33792 | tf_op jit(solution)/shard_map/all_gather | solution.py:171
  94.1 19.4 %fusion.63 = f32[8192,1536]{0,1:T(8,128)} fusion(s32[8192]{0:T(1024)S(1)} %fusion.124, bf16[64,512]{1,0:T(8,128)(2,1)S(1)} %get-tuple-element.55, bf16[64,512]{1,0:T(8,128)(2,1)S(1)} %get-tuple-element.54, bf16[64,512]{1,0:T(8,128)(2,1)S(1)} %get-tuple-element.53), kind=kOutput, calls=%fused_computation.120 | convolution fusion | flops 1611726848 | bytes 50561024 | tf_op jit(solution)/shard_map/dot_general | solution.py:141
  113.5 22.7 %slice_add_fusion.2 = f32[8192,512]{0,1:T(8,128)} fusion(f32[8192,1536]{0,1:T(8,128)} %fusion.63), kind=kLoop, calls=%fused_computation.16 | loop fusion | flops 8388608 | bytes 67108864 | tf_op jit(solution)/shard_map/add | solution.py:142
  136.3 9.1 copy.240
  145.4 17.5 %fusion.33 = f32[64,128,256]{2,0,1:T(8,128)} fusion(f32[64,128,256]{2,1,0:T(8,128)} %bitcast.127), kind=kOutput, calls=%fused_computation.66 | convolution fusion | flops 1610670080 | bytes 16777216 | tf_op jit(solution)/shard_map/abm,ca->cbm/dot_general | solution.py:45
  162.9 18.6 %multiply_subtract_fusion.3 = (f32[64,128,256]{2,0,1:T(8,128)S(1)}, f32[64,128,256]{2,0,1:T(8,128)}) fusion(f32[64,128,256]{2,0,1:T(8,128)} %fusion.33, f32[64,128]{0,1:T(8,128)S(1)} %get-tuple-element.64, f32[64,128]{0,1:T(8,128)S(1)} %get-tuple-element.65, f32[64,128,256]{2,1,0:T(8,128)} %bitcast.128), kind=kOutput, calls=%fused_computation.48 | convolution fusion | flops 1627451392 | bytes 33619968 | tf_op jit(solution)/shard_map/abm,ca->cbm/dot_general | solution.py:50
  181.5 17.5 %fusion.27 = f32[128,64,256]{2,0,1:T(8,128)} fusion(f32[64,128,256]{2,0,1:T(8,128)} %get-tuple-element.41), kind=kOutput, calls=%fused_computation.60 | convolution fusion | flops 3221454848 | bytes 16777216 | tf_op jit(solution)/shard_map/cbm,db->dcm/dot_general | solution.py:52
  199.0 13.5 %fusion.25 = f32[128,64,256]{2,0,1:T(8,128)} fusion(f32[64,128,256]{2,0,1:T(8,128)S(1)} %bitcast.130), kind=kOutput, calls=%fused_computation.58 | convolution fusion | flops 3221471232 | bytes 16777216 | tf_op jit(solution)/shard_map/cbm,db->dcm/dot_general | solution.py:47
  212.5 14.3 %fusion.45 = f32[128,64,256]{2,0,1:T(8,128)S(1)} fusion(f32[128,64,256]{2,0,1:T(8,128)} %fusion.27, f32[64,128,256]{2,0,1:T(8,128)S(1)} %get-tuple-element.40), kind=kOutput, calls=%fused_computation.94 | convolution fusion | flops 3223568384 | bytes 25165824 | tf_op jit(solution)/shard_map/cbm,db->dcm/dot_general | solution.py:50
  226.8 8.3 copy.249
  235.1 17.4 %subtract_add_fusion.1 = f32[128,64,256]{2,0,1:T(8,128)} fusion(f32[128,64,256]{2,0,1:T(8,128)} %fusion.25, f32[128,64,256]{2,0,1:T(8,128)S(1)} %fusion.45, f32[64,128,256]{2,0,1:T(8,128)S(1)} %get-tuple-element.40), kind=kOutput, calls=%fused_computation.46 | convolution fusion | flops 3227746304 | bytes 33554432 | tf_op jit(solution)/shard_map/cbm,db->dcm/dot_general | solution.py:45
  252.5 11.5 copy.247
  264.0 34.7 %gather_fusion = f32[8192,256]{1,0:T(8,128)} fusion(f32[8192,256]{1,0:T(8,128)} %bitcast.121, s32[8192]{0:T(1024)S(1)} %broadcast_clamp_fusion), kind=kCustom, calls=%fused_computation.clone | custom fusion | bytes 16809984 | tf_op jit(solution)/shard_map/jit(_take)/gather | solution.py:193
  298.8 8.9 copy.248
  307.6 34.7 %gather_fusion.1 = f32[8192,256]{1,0:T(8,128)} fusion(f32[8192,256]{1,0:T(8,128)} %bitcast.120, s32[8192]{0:T(1024)S(1)} %broadcast_clamp_fusion), kind=kCustom, calls=%fused_computation.1.clone | custom fusion | bytes 16809984 | tf_op jit(solution)/shard_map/jit(_take)/gather | solution.py:194
  342.4 8.9 copy.250
  351.3 19.2 %multiply_add_fusion.2 = (f32[8192,256]{0,1:T(8,128)}, f32[8192,256]{0,1:T(8,128)}) fusion(f32[8192,256]{0,1:T(8,128)} %copy.250, f32[8192,256]{0,1:T(8,128)} %copy.248, f32[8192,512]{0,1:T(8,128)} %slice_add_fusion.2, pred[8192]{0:T(1024)(128)(4,1)S(1)} %get-tuple-element.30), kind=kLoop, calls=%fused_computation.45 | loop fusion | flops 16777216 | bytes 50339840 | tf_op jit(solution)/shard_map/add | solution.py:195
  370.5 17.2 %fusion.104 = f32[8192,128]{1,0:T(8,128)S(1)} fusion(f32[8192,256]{0,1:T(8,128)} %get-tuple-element.36, s32[256]{0:T(256)S(1)} %copy-done.16), kind=kOutput, calls=%fused_computation.183 | convolution fusion | flops 3221684224 | bytes 12583936 | tf_op jit(solution)/shard_map/dot_general | solution.py:197
  387.8 14.6 %fusion.102 = f32[8192,128]{1,0:T(8,128)S(1)} fusion(f32[8192,256]{0,1:T(8,128)S(1)} %copy-done.2, s32[256]{0:T(256)S(1)} %copy-done.16), kind=kOutput, calls=%fused_computation.182 | convolution fusion | flops 3221684224 | bytes 12583936 | tf_op jit(solution)/shard_map/dot_general | solution.py:200
  402.4 14.8 %fusion.9 = f32[8192,1,128]{2,0,1:T(8,128)S(1)} fusion(f32[8192,128]{1,0:T(8,128)S(1)} %fusion.104, f32[8192,256]{0,1:T(8,128)S(1)} %copy-done.2, s32[256]{0:T(256)S(1)} %copy-done.16), kind=kOutput, calls=%fused_computation.25 | convolution fusion | flops 3222732800 | bytes 16778240 | tf_op jit(solution)/shard_map/dot_general | solution.py:197
  417.2 14.6 %fusion.8 = f32[8192,1,128]{2,0,1:T(8,128)S(1)} fusion(f32[8192,128]{1,0:T(8,128)S(1)} %fusion.102, f32[8192,256]{0,1:T(8,128)S(1)} %bitcast.123, s32[256]{0:T(256)S(1)} %copy-done.16), kind=kOutput, calls=%fused_computation.23 | convolution fusion | flops 3222732800 | bytes 16778240 | tf_op jit(solution)/shard_map/dot_general | solution.py:200
  432.3 31.2 %copy.251 = f32[8192,2,128]{2,1,0:T(2,128)S(1)} copy(f32[8192,2,128]{2,0,1:T(8,128)S(1)} %pad_maximum_fusion.2) | data formatting | bytes 16777216 | tf_op jit(solution)/shard_map/stack | solution.py:203
  463.5 97.4 %all_to_all.39 = f32[8192,2,128]{2,1,0:T(2,128)} all-to-all(f32[8192,2,128]{2,1,0:T(2,128)S(1)} %copy.251), channel_id=1, replica_groups=mesh['vis'=8,'tile'=4] {'vis'}, dimensions={0} | all-to-all | bytes 16777216 | tf_op jit(solution)/shard_map/all_to_all | solution.py:204
  560.9 7.4 reduce_sum.36
  573.2 24.1 %all-to-all-done.2 = f32[1024,2,128]{2,1,0:T(2,128)S(1)} async-done(((f32[1024,2,128]{2,1,0:T(2,128)}), f32[1024,2,128]{2,1,0:T(2,128)S(1)}, u32[]{:S(2)}, u32[]{:S(2)}) %all-to-all-start.2) | async-done | bytes 1048608 | tf_op jit(solution)/shard_map/all_to_all | solution.py:206
  598.9 37.5 %all-reduce = (f32[]{:T(128)}, f32[]{:T(128)}) all-reduce(f32[]{:T(128)} %fusion.168, f32[]{:T(128)} %get-tuple-element.60), channel_id=1, replica_groups=mesh['vis'=8,'tile'=4] {'vis','tile'}, use_global_device_ids=true, to_apply=%region_3.5 | all-reduce | flops 2 | bytes 16 | tf_op jit(solution)/shard_map/psum | solution.py:213
  639.7 29.3 %all-gather.4.cloned.1.call-done = f32[1024,2,128]{2,0,1:T(8,128)} async-done(((f32[256,2,128]{2,0,1:T(8,128)}), f32[1024,2,128]{2,0,1:T(8,128)}) %all-gather.4.cloned.1.call-update) | async-done | bytes 1048592 | tf_op jit(solution)/shard_map/all_gather | solution.py:218
  671.8 8.6 fusion.256
  684.5 18.9 %slice.172 = f32[1024,1027]{0,1:T(8,128)} slice(f32[1024,2054]{0,1:T(8,128)} %pad_maximum_fusion.1), slice={[0:1024:1], [0:2054:2]} | slice | bytes 8413184 | tf_op jit(solution)/shard_map/slice | solution.py:100
  703.4 18.8 %slice.174 = f32[1024,1027]{0,1:T(8,128)} slice(f32[1024,2054]{0,1:T(8,128)} %pad_maximum_fusion.1), slice={[0:1024:1], [1:2054:2]} | slice | bytes 8413184 | tf_op jit(solution)/shard_map/slice | solution.py:100
  722.2 13.6 %multiply_add_fusion.5 = f32[1024,1024]{0,1:T(8,128)S(1)} fusion(f32[1024,1027]{0,1:T(8,128)} %slice.174, f32[1024,1027]{0,1:T(8,128)} %slice.172), kind=kLoop, calls=%fused_computation.91 | loop fusion | flops 15728640 | bytes 37748736 | tf_op jit(solution)/shard_map/add | solution.py:107
  755.9 10.1 slice.184
  765.9 10.1 slice.186
  776.0 10.0 fusion.44
  786.0 10.1 fusion.43
  796.0 10.6 convolution_subtract_fusion
  806.6 22.0 %multiply_subtract_fusion.1 = (f32[8192,256]{0,1:T(8,128)}, f32[8192,256]{0,1:T(8,128)}) fusion(f32[8192,256]{0,1:T(8,128)} %convolution_subtract_fusion, f32[8192,512]{0,1:T(8,128)} %slice_add_fusion.2, f32[8192,256]{0,1:T(8,128)} %fusion.43, s32[256]{0:T(256)S(1)} %copy-done.16, f32[8192,2,128]{2,0,1:T(8,128)} %all-gather.6.cloned.1.call-done), kind=kOutput, calls=%fused_computation.43 | convolution fusion | flops 3236364288 | bytes 54526976 | tf_op jit(solution)/shard_map/dot_general | solution.py:223
  828.6 11.7 pad_maximum_fusion
  840.3 17.5 %copy.276 = f32[8192,512]{1,0:T(8,128)} copy(f32[8192,512]{0,1:T(8,128)} %pad_maximum_fusion) | data formatting | bytes 33554432 | tf_op jit(solution)/shard_map/reshape | solution.py:229
  857.8 10.4 reduce-precision_convert_fusion.1
  868.2 31.5 %fusion = f32[8,1024,1536]{2,1,0:T(8,128)} fusion(bf16[8,1024,512]{2,1,0:T(8,128)(2,1)S(1)} %get-tuple-element.45, bf16[8,1024,512]{2,1,0:T(8,128)(2,1)} %get-tuple-element.46, bf16[8,1024,512]{2,1,0:T(8,128)(2,1)S(1)} %get-tuple-element.44, s32[8,1024]{1,0:T(8,128)S(1)} %eq.45), kind=kOutput, calls=%fused_computation.3 | convolution fusion | flops 25853689856 | bytes 75530240 | tf_op jit(solution)/shard_map/gkb,gbc->gkc/dot_general | solution.py:151
  899.7 23.9 %slice_add_fusion = f32[8,1024,512]{2,1,0:T(8,128)} fusion(f32[8,1024,1536]{2,1,0:T(8,128)} %fusion), kind=kLoop, calls=%fused_computation.14 | loop fusion | flops 8388608 | bytes 67108864 | tf_op jit(solution)/shard_map/add | solution.py:152
  930.0 13.2 %fusion.17 = f32[64,128,256]{2,0,1:T(8,128)} fusion(f32[64,128,256]{2,1,0:T(8,128)S(1)} %bitcast.131), kind=kOutput, calls=%fused_computation.50 | convolution fusion | flops 1610670080 | bytes 16777216 | tf_op jit(solution)/shard_map/abm,ca->cbm/dot_general | solution.py:47
  943.2 13.6 %fusion.19 = f32[64,128,256]{2,0,1:T(8,128)} fusion(f32[64,128,256]{2,1,0:T(8,128)S(1)} %bitcast.132), kind=kOutput, calls=%fused_computation.52 | convolution fusion | flops 1610670080 | bytes 16777216 | tf_op jit(solution)/shard_map/abm,ca->cbm/dot_general | solution.py:52
  956.8 13.2 %fusion.23 = f32[64,128,256]{2,0,1:T(8,128)} fusion(f32[64,128,256]{2,1,0:T(8,128)S(1)} %bitcast.133), kind=kOutput, calls=%fused_computation.56 | convolution fusion | flops 1610670080 | bytes 16777216 | tf_op jit(solution)/shard_map/abm,ca->cbm/dot_general | solution.py:50
  969.9 21.5 %multiply_subtract_fusion = (f32[64,128,256]{2,0,1:T(8,128)}, f32[64,128,256]{2,0,1:T(8,128)}) fusion(f32[64,128,256]{2,0,1:T(8,128)} %fusion.17, f32[64,128]{0,1:T(8,128)S(1)} %copy-done.12, f32[64,128]{0,1:T(8,128)S(1)} %copy-done.9, f32[64,128,256]{2,0,1:T(8,128)} %fusion.23, f32[64,128,256]{2,0,1:T(8,128)} %fusion.19, f32[64,128,256]{2,1,0:T(8,128)S(1)} %bitcast.134), kind=kOutput, calls=%fused_computation.40 | convolution fusion | flops 1631641600 | bytes 50397184 | tf_op jit(solution)/shard_map/abm,ca->cbm/dot_general | solution.py:45
  991.5 16.3 %fusion.13 = f32[128,64,256]{2,0,1:T(8,128)S(1)} fusion(f32[64,128,256]{2,0,1:T(8,128)} %get-tuple-element.35), kind=kOutput, calls=%fused_computation.34 | convolution fusion | flops 3221454848 | bytes 16777216 | tf_op jit(solution)/shard_map/cbm,db->dcm/dot_general | solution.py:47
  1007.8 11.8 fusion.50
  1019.7 8.3 copy.264
  1047.6 20.8 %fusion.42 = (f32[1024,1024]{0,1:T(8,128)}, f32[1024,1024]{0,1:T(8,128)}) fusion(f32[1024,1024]{0,1:T(8,128)} %mul.725, f32[1,1024,1024]{1,2,0:T(8,128)} %copy.279, f32[1024,1027]{0,1:T(8,128)} %slice.174, f32[1024,1027]{0,1:T(8,128)} %slice.172, f32[1,1024,1024]{1,2,0:T(8,128)} %copy.278), kind=kLoop, calls=%fused_computation.90 | loop fusion | flops 25165824 | bytes 54525952 | tf_op jit(solution)/shard_map/mul | solution.py:240
  1068.4 8.8 fusion.41
  1077.2 9.8 slice.194
  1087.0 9.8 slice.195
  1100.0 9.4 copy.272
  1124.7 8.4 pad_maximum_fusion.4
  1133.1 8.9 copy.275
  1142.0 20.7 %add_bitcast_fusion.1 = (f32[1024,1024,1]{0,1,2:T(8,128)S(1)}, f32[1024,1024,1]{0,1,2:T(8,128)S(1)}) fusion(f32[1024,1024]{0,1:T(8,128)} %reshape.132, f32[1024,1024]{0,1:T(8,128)} %get-tuple-element.32, f32[1024,3]{0,1:T(4,128)S(1)} %get-tuple-element.57, f32[1024,3]{0,1:T(4,128)S(1)} %get-tuple-element.56), kind=kLoop, calls=%fused_computation.87 | loop fusion | flops 41943040 | bytes 16801792 | tf_op jit(solution)/shard_map/stack | solution.py:124
  1164.4 13.0 %copy.271 = f32[1024,1024,2]{0,2,1:T(2,128)} copy(f32[1024,1024,2]{0,1,2:T(8,128)S(1)} %pad_maximum_fusion.3) | data formatting | bytes 16777216 | tf_op jit(solution)/shard_map/stack | solution.py:124
  1177.4 11.0 reshape.133
  1189.2 7.5 multiply_bitcast_fusion
  1196.7 9.2 copy.265
  1205.9 13.6 %fusion.12 = f32[1024,2048]{0,1:T(8,128)} fusion(f32[1024,2048]{0,1:T(8,128)} %copy.272, f32[1024,2048]{0,1:T(8,128)} %reshape.133, f32[1024,8,256]{0,2,1:T(8,128)} %copy.265), kind=kLoop, calls=%fused_computation.33 | loop fusion | flops 8388608 | bytes 33554432 | tf_op jit(solution)/shard_map/max | solution.py:250
  1219.5 9.1 copy.273
  (112 shorter events, 88.8 us)
Async XLA Ops:
  7.2 590.7 %copy-start = (f32[128,128]{1,0:T(8,128)S(1)}, f32[128,128]{1,0:T(8,128)}, u32[]{:S(2)}) copy-start(f32[128,128]{1,0:T(8,128)} %param.15) | copy-start | bytes 196612
  16.5 5.3 copy-start.17
  16.5 119.8 %all-to-all-start = ((f32[1024,8,256]{0,2,1:T(8,128)}), f32[1024,8,256]{0,2,1:T(8,128)}, u32[]{:S(2)}, u32[]{:S(2)}) async-start(f32[1024,8,256]{0,2,1:T(8,128)} %bitcast.124), calls=%async_computation | async-start | bytes 16777216 | tf_op jit(solution)/shard_map/all_to_all | solution.py:169
  92.8 0.7 copy-start.15
  93.0 69.9 %copy-start.8 = (f32[64,128]{0,1:T(8,128)}, f32[64,128]{0,1:T(8,128)S(1)}, u32[]{:S(2)}) copy-start(f32[64,128]{0,1:T(8,128)S(1)} %get-tuple-element.65) | copy-start | bytes 98308
  93.5 0.6 copy-start.10
  181.5 17.5 %slice-start.4 = ((s8[8388608]{0:T(1024)(128)(4,1)}), s8[4194304]{0:T(1024)(128)(4,1)S(1)}, s32[]{:S(2)}) async-start(s8[8388608]{0:T(1024)(128)(4,1)} %bitcast.129), calls=%async_computation.10 | async-start | bytes 8388608
  181.5 17.5 %slice-start.5 = ((s8[8388608]{0:T(1024)(128)(4,1)}), s8[4194304]{0:T(1024)(128)(4,1)S(1)}, s32[]{:S(2)}) async-start(s8[8388608]{0:T(1024)(128)(4,1)} %bitcast.129), calls=%async_computation.11 | async-start | bytes 8388608
  351.3 19.2 %copy-start.16 = (s32[256]{0:T(256)S(1)}, s32[256]{0:T(256)}, u32[]{:S(2)}) copy-start(s32[256]{0:T(256)} %copy-done.15) | copy-start | bytes 3076
  370.5 17.2 %copy-start.2 = (f32[8192,256]{0,1:T(8,128)S(1)}, f32[8192,256]{0,1:T(8,128)}, u32[]{:S(2)}) copy-start(f32[8192,256]{0,1:T(8,128)} %get-tuple-element.37) | copy-start | bytes 25165828
  387.8 29.4 %slice-start = ((s8[8388608]{0:T(1024)(128)(4,1)}), s8[4194304]{0:T(1024)(128)(4,1)S(1)}, s32[]{:S(2)}) async-start(s8[8388608]{0:T(1024)(128)(4,1)} %bitcast.122), calls=%async_computation.6 | async-start | bytes 8388608
  402.3 14.8 %slice-start.1 = ((s8[8388608]{0:T(1024)(128)(4,1)}), s8[4194304]{0:T(1024)(128)(4,1)S(1)}, s32[]{:S(2)}) async-start(s8[8388608]{0:T(1024)(128)(4,1)} %bitcast.122), calls=%async_computation.7 | async-start | bytes 8388608
  560.9 37.0 %copy-start.13 = (f32[256,2,128]{2,1,0:T(2,128)S(1)}, f32[256,2,128]{2,1,0:T(2,128)}, u32[]{:S(2)}) copy-start(f32[256,2,128]{2,1,0:T(2,128)} %param.14) | copy-start | bytes 786436
  560.9 37.0 %copy-start.14 = (f32[256,2,128]{2,1,0:T(2,128)S(1)}, f32[256,2,128]{2,1,0:T(2,128)}, u32[]{:S(2)}) copy-start(f32[256,2,128]{2,1,0:T(2,128)} %param.12) | copy-start | bytes 786436
  568.4 28.9 %all-to-all-start.2 = ((f32[1024,2,128]{2,1,0:T(2,128)}), f32[1024,2,128]{2,1,0:T(2,128)S(1)}, u32[]{:S(2)}, u32[]{:S(2)}) async-start(f32[1024,2,128]{2,1,0:T(2,128)} %reduce_sum.36), calls=%async_computation.2 | async-start | bytes 2097152 | tf_op jit(solution)/shard_map/all_to_all | solution.py:206
  571.9 97.1 %all-gather.4.cloned.1.call-start = ((), (), s32[]{:S(2)}) async-start(), calls=%async_computation.4 | async-start | bytes 1310720 | tf_op jit(solution)/shard_map/all_gather | solution.py:218
  637.8 0.7 copy-start.6
  639.6 136.3 %all-gather.6.cloned.1.call-start = ((), (), s32[]{:S(2)}) async-start(), calls=%async_computation.5 | async-start | bytes 9437184 | tf_op jit(solution)/shard_map/all_gather | solution.py:219
  669.0 11.3 slice-start.2
  670.0 10.4 slice-start.3
  670.0 10.4 collective-permute-start
  722.2 18.0 %copy-start.11 = (s32[8192]{0:T(1024)S(1)}, s32[8192]{0:T(1024)}, u32[]{:S(2)}) copy-start(s32[8192]{0:T(1024)} %copy-done.10) | copy-start | bytes 98308
  735.9 2.0 copy-start.5
  737.9 13.2 %collective-permute-start.1 = (f32[1024,6]{0,1:T(8,128)S(1)}, f32[1024,6]{0,1:T(8,128)S(1)}, u32[]{:S(2)}, u32[]{:S(2)}) collective-permute-start(f32[1024,6]{0,1:T(8,128)S(1)} %slice.235), channel_id=1, source_target_pairs={{1,0},{2,1},{3,2},{0,3},{5,4},{6,5},{7,6},{4,7},{9,8},{10,9},{11,1... | collective-permute-start | bytes 73736 | tf_op jit(solution)/shard_map/ppermute | solution.py:26
  776.0 10.0 copy-start.3
  956.8 13.2 %copy-start.9 = (f32[64,128]{0,1:T(8,128)S(1)}, f32[64,128]{0,1:T(8,128)}, u32[]{:S(2)}) copy-start(f32[64,128]{0,1:T(8,128)} %copy-done.8) | copy-start | bytes 98308
  956.8 13.2 %copy-start.12 = (f32[64,128]{0,1:T(8,128)S(1)}, f32[64,128]{0,1:T(8,128)}, u32[]{:S(2)}) copy-start(f32[64,128]{0,1:T(8,128)} %fusion.138) | copy-start | bytes 98308
  991.5 16.3 %slice-start.6 = ((s8[8388608]{0:T(1024)(128)(4,1)}), s8[4194304]{0:T(1024)(128)(4,1)S(1)}, s32[]{:S(2)}) async-start(s8[8388608]{0:T(1024)(128)(4,1)} %bitcast.140), calls=%async_computation.12 | async-start | bytes 8388608
  991.5 16.3 %slice-start.7 = ((s8[8388608]{0:T(1024)(128)(4,1)}), s8[4194304]{0:T(1024)(128)(4,1)S(1)}, s32[]{:S(2)}) async-start(s8[8388608]{0:T(1024)(128)(4,1)} %bitcast.140), calls=%async_computation.13 | async-start | bytes 8388608
  1027.9 5.1 copy-start.4
  1028.0 161.3 %all-to-all-start.3 = ((f32[8,1024,256]{2,1,0:T(8,128)}), f32[8,1024,256]{2,1,0:T(8,128)}, u32[]{:S(2)}, u32[]{:S(2)}) async-start(f32[8,1024,256]{2,1,0:T(8,128)} %bitcast.139), calls=%async_computation.3 | async-start | bytes 16777216 | tf_op jit(solution)/shard_map/all_to_all | solution.py:233
  1099.4 10.0 collective-permute-start.2
  1123.5 18.5 %collective-permute-start.3 = (f32[2,1024,3]{1,2,0:T(4,128)S(1)}, f32[2,1024,3]{1,2,0:T(4,128)S(1)}, u32[]{:S(2)}, u32[]{:S(2)}) collective-permute-start(f32[2,1024,3]{1,2,0:T(4,128)S(1)} %pad_maximum_fusion.11), channel_id=1, source_target_pairs={{3,0},{0,1},{1,2},{2,3},{7,4},{4,5},{5,6},{6,7},{11,8},{8,9},{9,10... | collective-permute-start | bytes 73736 | tf_op jit(solution)/shard_map/ppermute | solution.py:26
  1177.4 11.0 copy-start.7
  1205.9 22.8 %copy-start.1 = (f32[128,128]{1,0:T(8,128)S(1)}, f32[128,128]{1,0:T(8,128)}, u32[]{:S(2)}) copy-start(f32[128,128]{1,0:T(8,128)} %param.15) | copy-start | bytes 196612
Sparse Core Ops, SparseCore 0:
  639.8 29.2 all-gather.3
  670.9 53.6 all-gather.5
where the time goes:
time: 1250 us; the launch traced here: 1240 us
  local copies, waits for them, and re-layouts  373 us (30%)
  matrix products  355 us (28%)
  other arithmetic  212 us (17%)
  blocking collectives  206 us (16%)
  waiting for transfers between devices  53.5 us (4%)
  starting transfers between devices  19 us (2%)
  between operations  17 us (1%)
    all_to_all x1, blocking collectives, on_device(): lax.all_to_all(partial, 'vis', split_axis=0, concat_axis=0, tiled=True)  97.4 us
    all_gather x1, blocking collectives, on_device(): all_index = lax.all_gather(block_index, ('vis', 'tile'), tiled=True)  70.9 us
    dot_general x4, matrix products, complex_einsum(): real_part = jnp.einsum(form, left_real, table_cos, precision=precise)  68.3 us
    slice x4, local copies, waits for them, and re-layouts, analyse_local(): lax.slice_in_dim(extended, parity, extended.shape[1], 2, 1)  57.8 us
    unnamed x59, local copies, waits for them, and re-layouts  51.8 us
    dot_general x3, matrix products, complex_einsum(): imag_part = jnp.einsum(form, left_real, table_sin, precision=precise)  46 us
    gather x2, local copies, waits for them, and re-layouts, on_device(): picked_imag = jnp.take(spec_imag, row_of, axis=0)  43.6 us
    gather x2, local copies, waits for them, and re-layouts, on_device(): picked_real = jnp.take(spec_real, row_of, axis=0)  43.6 us
  transfers between devices with their start and end apart: 9, of which 2 were waited for; matrix products, arithmetic and copies ran while one was open for 24% of the time, Pallas kernels for 0%

commit v1 on v0

--- a/solution.py
+++ b/solution.py
@@ -18,6 +18,18 @@
     ((1.0 if position % 2 == 0 else -1.0) * LOW_TAPS[7 - position] for position in range(8))
 )
 TWO_PI = 2.0 * math.pi
+
+
+def collect(x, axis, dim):
+    ways, here, lap = (lax.axis_size(axis), lax.axis_index(axis), x.shape[dim])
+    line, have = (x, 1)
+    while have < ways:
+        line = jnp.concatenate(
+            [line, lax.ppermute(line, axis, [(d, (d - have) % ways) for d in range(ways)])],
+            axis=dim,
+        )
+        have = 2 * have
+    return jnp.roll(line, here * lap, axis=dim)
 
 
 def shifted(block, axis, distance):
@@ -168,7 +180,7 @@
     norm_scale = 1.0 / math.sqrt(len_rows * len_cols)
     columns = lax.all_to_all(extrapolated, "vis", split_axis=1, concat_axis=0, tiled=True)
     spec_real, spec_imag = transform_axis(columns, None, -1.0, 0, False)
-    all_index = lax.all_gather(block_index, ("vis", "tile"), tiled=True)
+    all_index = collect(block_index, ("vis", "tile"), 0)
     total_blocks = all_index.shape[0]
     owner = jnp.arange(total_blocks, dtype=jnp.int32) // slot_count
     per_row = slab_cols // block_width

time: 1250 us -> 1290 us (1.032)
  waiting for transfers between devices: 53.5 us -> 145 us
  blocking collectives: 206 us -> 136 us
    ppermute x0 -> x5, waiting for transfers between devices: none -> 91.9 us  [collect(): lax.ppermute(line, axis, [(d, (d - have) % ways) for d in range(ways)])]
    all_gather x1 -> x0, blocking collectives: 70.9 us -> none  [on_device(): all_index = lax.all_gather(block_index, ('vis', 'tile'), tiled=True)]
    unnamed x59 -> x69, local copies, waits for them, and re-layouts: 51.8 us -> 52.4 us
  transfers between devices with their start and end apart: 9 -> 14, of which waited for: 2 -> 6; matrix products, arithmetic and copies ran while one was open for 24% -> 24% of each run, Pallas kernels for 0% -> 0%
where the time goes in v1:
time: 1290 us; the launch traced here: 1270 us
  local copies, waits for them, and re-layouts  374 us (29%)
  matrix products  355 us (28%)
  other arithmetic  213 us (17%)
  waiting for transfers between devices  145 us (11%)
  blocking collectives  136 us (11%)
  starting transfers between devices  30.6 us (2%)
  between operations  17.1 us (1%)
    all_to_all x1, blocking collectives, on_device(): lax.all_to_all(partial, 'vis', split_axis=0, concat_axis=0, tiled=True)  98.3 us
    ppermute x5, waiting for transfers between devices, collect(): lax.ppermute(line, axis, [(d, (d - have) % ways) for d in range(ways)])  91.9 us
    dot_general x4, matrix products, complex_einsum(): real_part = jnp.einsum(form, left_real, table_cos, precision=precise)  68.4 us
    slice x4, local copies, waits for them, and re-layouts, analyse_local(): lax.slice_in_dim(extended, parity, extended.shape[1], 2, 1)  58.1 us
    unnamed x69, local copies, waits for them, and re-layouts  52.4 us
    dot_general x3, matrix products, complex_einsum(): imag_part = jnp.einsum(form, left_real, table_sin, precision=precise)  46 us
    gather x2, local copies, waits for them, and re-layouts, on_device(): picked_real = jnp.take(spec_real, row_of, axis=0)  43.9 us
    gather x2, local copies, waits for them, and re-layouts, on_device(): picked_imag = jnp.take(spec_imag, row_of, axis=0)  43.8 us
  transfers between devices with their start and end apart: 14, of which 6 were waited for; matrix products, arithmetic and copies ran while one was open for 24% of the time, Pallas kernels for 0%

profile of v1, /device:TPU:0, one launch (start us, length us, event | category | flops | bytes accessed | tf_op | source)
XLA Modules:
  0.0 1271.4 jit_solution(12820349280067109435)
XLA Ops:
  13.6 9.2 copy.239
  35.0 84.1 %collective-permute-done.2 = s32[1024]{0:T(1024)S(1)} collective-permute-done((s32[1024]{0:T(1024)S(1)}, s32[1024]{0:T(1024)S(1)}, u32[]{:S(2)}, u32[]{:S(2)}) %collective-permute-start.2) | collective-permute-done | bytes 4128 | tf_op jit(solution)/shard_map/ppermute | solution.py:28
  127.6 19.4 %fusion.63 = f32[8192,1536]{0,1:T(8,128)} fusion(s32[8192]{0:T(1024)S(1)} %get-tuple-element.77, bf16[64,512]{1,0:T(8,128)(2,1)S(1)} %get-tuple-element.56, bf16[64,512]{1,0:T(8,128)(2,1)S(1)} %get-tuple-element.55, bf16[64,512]{1,0:T(8,128)(2,1)S(1)} %get-tuple-element.54), kind=kOutput, calls=%fused_computation.120 | convolution fusion | flops 1611726848 | bytes 50561024 | tf_op jit(solution)/shard_map/dot_general | solution.py:153
  147.0 22.7 %slice_add_fusion.2 = f32[8192,512]{0,1:T(8,128)} fusion(f32[8192,1536]{0,1:T(8,128)} %fusion.63), kind=kLoop, calls=%fused_computation.16 | loop fusion | flops 8388608 | bytes 67108864 | tf_op jit(solution)/shard_map/add | solution.py:154
  169.7 9.1 copy.240
  178.8 17.6 %fusion.33 = f32[64,128,256]{2,0,1:T(8,128)} fusion(f32[64,128,256]{2,1,0:T(8,128)} %bitcast.125), kind=kOutput, calls=%fused_computation.66 | convolution fusion | flops 1610670080 | bytes 16777216 | tf_op jit(solution)/shard_map/abm,ca->cbm/dot_general | solution.py:57
  196.4 18.5 %multiply_subtract_fusion.3 = (f32[64,128,256]{2,0,1:T(8,128)S(1)}, f32[64,128,256]{2,0,1:T(8,128)}) fusion(f32[64,128,256]{2,0,1:T(8,128)} %fusion.33, f32[64,128]{0,1:T(8,128)S(1)} %get-tuple-element.75, f32[64,128]{0,1:T(8,128)S(1)} %get-tuple-element.76, f32[64,128,256]{2,1,0:T(8,128)} %bitcast.126), kind=kOutput, calls=%fused_computation.48 | convolution fusion | flops 1627451392 | bytes 33619968 | tf_op jit(solution)/shard_map/abm,ca->cbm/dot_general | solution.py:62
  215.0 17.5 %fusion.27 = f32[128,64,256]{2,0,1:T(8,128)} fusion(f32[64,128,256]{2,0,1:T(8,128)} %get-tuple-element.42), kind=kOutput, calls=%fused_computation.60 | convolution fusion | flops 3221454848 | bytes 16777216 | tf_op jit(solution)/shard_map/cbm,db->dcm/dot_general | solution.py:64
  232.5 13.5 %fusion.25 = f32[128,64,256]{2,0,1:T(8,128)} fusion(f32[64,128,256]{2,0,1:T(8,128)S(1)} %bitcast.128), kind=kOutput, calls=%fused_computation.58 | convolution fusion | flops 3221471232 | bytes 16777216 | tf_op jit(solution)/shard_map/cbm,db->dcm/dot_general | solution.py:59
  246.1 14.3 %fusion.45 = f32[128,64,256]{2,0,1:T(8,128)S(1)} fusion(f32[128,64,256]{2,0,1:T(8,128)} %fusion.27, f32[64,128,256]{2,0,1:T(8,128)S(1)} %get-tuple-element.41), kind=kOutput, calls=%fused_computation.94 | convolution fusion | flops 3223568384 | bytes 25165824 | tf_op jit(solution)/shard_map/cbm,db->dcm/dot_general | solution.py:62
  260.4 8.3 copy.249
  268.6 17.4 %subtract_add_fusion.1 = f32[128,64,256]{2,0,1:T(8,128)} fusion(f32[128,64,256]{2,0,1:T(8,128)} %fusion.25, f32[128,64,256]{2,0,1:T(8,128)S(1)} %fusion.45, f32[64,128,256]{2,0,1:T(8,128)S(1)} %get-tuple-element.41), kind=kOutput, calls=%fused_computation.46 | convolution fusion | flops 3227746304 | bytes 33554432 | tf_op jit(solution)/shard_map/cbm,db->dcm/dot_general | solution.py:57
  286.1 11.5 copy.247
  297.6 34.9 %gather_fusion = f32[8192,256]{1,0:T(8,128)} fusion(f32[8192,256]{1,0:T(8,128)} %bitcast.119, s32[8192]{0:T(1024)S(1)} %get-tuple-element.78), kind=kCustom, calls=%fused_computation.clone | custom fusion | bytes 16809984 | tf_op jit(solution)/shard_map/jit(_take)/gather | solution.py:205
  332.5 9.0 copy.248
  341.5 34.9 %gather_fusion.1 = f32[8192,256]{1,0:T(8,128)} fusion(f32[8192,256]{1,0:T(8,128)} %bitcast.118, s32[8192]{0:T(1024)S(1)} %get-tuple-element.78), kind=kCustom, calls=%fused_computation.1.clone | custom fusion | bytes 16809984 | tf_op jit(solution)/shard_map/jit(_take)/gather | solution.py:206
  376.4 8.9 copy.250
  385.3 19.3 %multiply_add_fusion.2 = (f32[8192,256]{0,1:T(8,128)}, f32[8192,256]{0,1:T(8,128)}) fusion(f32[8192,256]{0,1:T(8,128)} %copy.250, f32[8192,256]{0,1:T(8,128)} %copy.248, f32[8192,512]{0,1:T(8,128)} %slice_add_fusion.2, pred[8192]{0:T(1024)(128)(4,1)S(1)} %get-tuple-element.30), kind=kLoop, calls=%fused_computation.45 | loop fusion | flops 16777216 | bytes 50339840 | tf_op jit(solution)/shard_map/add | solution.py:207
  404.6 17.2 %fusion.104 = f32[8192,128]{1,0:T(8,128)S(1)} fusion(f32[8192,256]{0,1:T(8,128)} %get-tuple-element.37, s32[256]{0:T(256)S(1)} %copy-done.16), kind=kOutput, calls=%fused_computation.183 | convolution fusion | flops 3221684224 | bytes 12583936 | tf_op jit(solution)/shard_map/dot_general | solution.py:209
  421.9 14.6 %fusion.102 = f32[8192,128]{1,0:T(8,128)S(1)} fusion(f32[8192,256]{0,1:T(8,128)S(1)} %copy-done.2, s32[256]{0:T(256)S(1)} %copy-done.16), kind=kOutput, calls=%fused_computation.182 | convolution fusion | flops 3221684224 | bytes 12583936 | tf_op jit(solution)/shard_map/dot_general | solution.py:212
  436.5 14.8 %fusion.9 = f32[8192,1,128]{2,0,1:T(8,128)S(1)} fusion(f32[8192,128]{1,0:T(8,128)S(1)} %fusion.104, f32[8192,256]{0,1:T(8,128)S(1)} %copy-done.2, s32[256]{0:T(256)S(1)} %copy-done.16), kind=kOutput, calls=%fused_computation.25 | convolution fusion | flops 3222732800 | bytes 16778240 | tf_op jit(solution)/shard_map/dot_general | solution.py:209
  451.3 14.6 %fusion.8 = f32[8192,1,128]{2,0,1:T(8,128)S(1)} fusion(f32[8192,128]{1,0:T(8,128)S(1)} %fusion.102, f32[8192,256]{0,1:T(8,128)S(1)} %bitcast.121, s32[256]{0:T(256)S(1)} %copy-done.16), kind=kOutput, calls=%fused_computation.23 | convolution fusion | flops 3222732800 | bytes 16778240 | tf_op jit(solution)/shard_map/dot_general | solution.py:212
  466.4 31.2 %copy.251 = f32[8192,2,128]{2,1,0:T(2,128)S(1)} copy(f32[8192,2,128]{2,0,1:T(8,128)S(1)} %pad_maximum_fusion.2) | data formatting | bytes 16777216 | tf_op jit(solution)/shard_map/stack | solution.py:215
  497.6 98.3 %all_to_all.39 = f32[8192,2,128]{2,1,0:T(2,128)} all-to-all(f32[8192,2,128]{2,1,0:T(2,128)S(1)} %copy.251), channel_id=1, replica_groups=mesh['vis'=8,'tile'=4] {'vis'}, dimensions={0} | all-to-all | bytes 16777216 | tf_op jit(solution)/shard_map/all_to_all | solution.py:216
  595.9 7.4 reduce_sum.36
  608.2 24.1 %all-to-all-done.2 = f32[1024,2,128]{2,1,0:T(2,128)S(1)} async-done(((f32[1024,2,128]{2,1,0:T(2,128)}), f32[1024,2,128]{2,1,0:T(2,128)S(1)}, u32[]{:S(2)}, u32[]{:S(2)}) %all-to-all-start.2) | async-done | bytes 1048608 | tf_op jit(solution)/shard_map/all_to_all | solution.py:218
  633.9 37.5 %all-reduce = (f32[]{:T(128)}, f32[]{:T(128)}) all-reduce(f32[]{:T(128)} %fusion.168, f32[]{:T(128)} %get-tuple-element.71), channel_id=1, replica_groups=mesh['vis'=8,'tile'=4] {'vis','tile'}, use_global_device_ids=true, to_apply=%region_3.5 | all-reduce | flops 2 | bytes 16 | tf_op jit(solution)/shard_map/psum | solution.py:225
  674.7 29.3 %all-gather.3.cloned.1.call-done = f32[1024,2,128]{2,0,1:T(8,128)} async-done(((f32[256,2,128]{2,0,1:T(8,128)}), f32[1024,2,128]{2,0,1:T(8,128)}) %all-gather.3.cloned.1.call-update) | async-done | bytes 1048592 | tf_op jit(solution)/shard_map/all_gather | solution.py:230
  706.7 8.6 fusion.256
  719.5 19.0 %slice.172 = f32[1024,1027]{0,1:T(8,128)} slice(f32[1024,2054]{0,1:T(8,128)} %pad_maximum_fusion.1), slice={[0:1024:1], [0:2054:2]} | slice | bytes 8413184 | tf_op jit(solution)/shard_map/slice | solution.py:112
  738.5 19.0 %slice.174 = f32[1024,1027]{0,1:T(8,128)} slice(f32[1024,2054]{0,1:T(8,128)} %pad_maximum_fusion.1), slice={[0:1024:1], [1:2054:2]} | slice | bytes 8413184 | tf_op jit(solution)/shard_map/slice | solution.py:112
  757.5 13.5 %multiply_add_fusion.5 = f32[1024,1024]{0,1:T(8,128)S(1)} fusion(f32[1024,1027]{0,1:T(8,128)} %slice.174, f32[1024,1027]{0,1:T(8,128)} %slice.172), kind=kLoop, calls=%fused_computation.91 | loop fusion | flops 15728640 | bytes 37748736 | tf_op jit(solution)/shard_map/add | solution.py:119
  791.0 10.1 slice.184
  801.1 10.1 slice.186
  811.1 10.0 fusion.44
  821.2 10.1 fusion.43
  831.2 10.6 convolution_subtract_fusion
  841.8 22.0 %multiply_subtract_fusion.1 = (f32[8192,256]{0,1:T(8,128)}, f32[8192,256]{0,1:T(8,128)}) fusion(f32[8192,256]{0,1:T(8,128)} %convolution_subtract_fusion, f32[8192,512]{0,1:T(8,128)} %slice_add_fusion.2, f32[8192,256]{0,1:T(8,128)} %fusion.43, s32[256]{0:T(256)S(1)} %copy-done.16, f32[8192,2,128]{2,0,1:T(8,128)} %all-gather.5.cloned.1.call-done), kind=kOutput, calls=%fused_computation.43 | convolution fusion | flops 3236364288 | bytes 54526976 | tf_op jit(solution)/shard_map/dot_general | solution.py:235
  863.8 11.7 pad_maximum_fusion
  875.5 17.5 %copy.276 = f32[8192,512]{1,0:T(8,128)} copy(f32[8192,512]{0,1:T(8,128)} %pad_maximum_fusion) | data formatting | bytes 33554432 | tf_op jit(solution)/shard_map/reshape | solution.py:241
  893.0 10.4 reduce-precision_convert_fusion.1
  903.4 31.6 %fusion = f32[8,1024,1536]{2,1,0:T(8,128)} fusion(bf16[8,1024,512]{2,1,0:T(8,128)(2,1)S(1)} %get-tuple-element.46, bf16[8,1024,512]{2,1,0:T(8,128)(2,1)} %get-tuple-element.47, bf16[8,1024,512]{2,1,0:T(8,128)(2,1)S(1)} %get-tuple-element.45, s32[8,1024]{1,0:T(8,128)S(1)} %eq.48), kind=kOutput, calls=%fused_computation.3 | convolution fusion | flops 25853689856 | bytes 75530240 | tf_op jit(solution)/shard_map/gkb,gbc->gkc/dot_general | solution.py:163
  934.9 23.9 %slice_add_fusion = f32[8,1024,512]{2,1,0:T(8,128)} fusion(f32[8,1024,1536]{2,1,0:T(8,128)} %fusion), kind=kLoop, calls=%fused_computation.14 | loop fusion | flops 8388608 | bytes 67108864 | tf_op jit(solution)/shard_map/add | solution.py:164
  965.2 13.2 %fusion.17 = f32[64,128,256]{2,0,1:T(8,128)} fusion(f32[64,128,256]{2,1,0:T(8,128)S(1)} %bitcast.129), kind=kOutput, calls=%fused_computation.50 | convolution fusion | flops 1610670080 | bytes 16777216 | tf_op jit(solution)/shard_map/abm,ca->cbm/dot_general | solution.py:59
  978.4 13.6 %fusion.19 = f32[64,128,256]{2,0,1:T(8,128)} fusion(f32[64,128,256]{2,1,0:T(8,128)S(1)} %bitcast.130), kind=kOutput, calls=%fused_computation.52 | convolution fusion | flops 1610670080 | bytes 16777216 | tf_op jit(solution)/shard_map/abm,ca->cbm/dot_general | solution.py:64
  992.0 13.2 %fusion.23 = f32[64,128,256]{2,0,1:T(8,128)} fusion(f32[64,128,256]{2,1,0:T(8,128)S(1)} %bitcast.131), kind=kOutput, calls=%fused_computation.56 | convolution fusion | flops 1610670080 | bytes 16777216 | tf_op jit(solution)/shard_map/abm,ca->cbm/dot_general | solution.py:62
  1005.2 21.5 %multiply_subtract_fusion = (f32[64,128,256]{2,0,1:T(8,128)}, f32[64,128,256]{2,0,1:T(8,128)}) fusion(f32[64,128,256]{2,0,1:T(8,128)} %fusion.17, f32[64,128]{0,1:T(8,128)S(1)} %copy-done.12, f32[64,128]{0,1:T(8,128)S(1)} %copy-done.9, f32[64,128,256]{2,0,1:T(8,128)} %fusion.23, f32[64,128,256]{2,0,1:T(8,128)} %fusion.19, f32[64,128,256]{2,1,0:T(8,128)S(1)} %bitcast.132), kind=kOutput, calls=%fused_computation.40 | convolution fusion | flops 1631641600 | bytes 50397184 | tf_op jit(solution)/shard_map/abm,ca->cbm/dot_general | solution.py:57
  1026.8 16.3 %fusion.13 = f32[128,64,256]{2,0,1:T(8,128)S(1)} fusion(f32[64,128,256]{2,0,1:T(8,128)} %get-tuple-element.36), kind=kOutput, calls=%fused_computation.34 | convolution fusion | flops 3221454848 | bytes 16777216 | tf_op jit(solution)/shard_map/cbm,db->dcm/dot_general | solution.py:59
  1043.1 11.8 fusion.50
  1054.9 8.3 copy.264
  1082.9 20.8 %fusion.42 = (f32[1024,1024]{0,1:T(8,128)}, f32[1024,1024]{0,1:T(8,128)}) fusion(f32[1024,1024]{0,1:T(8,128)} %mul.733, f32[1,1024,1024]{1,2,0:T(8,128)} %copy.279, f32[1024,1027]{0,1:T(8,128)} %slice.174, f32[1024,1027]{0,1:T(8,128)} %slice.172, f32[1,1024,1024]{1,2,0:T(8,128)} %copy.278), kind=kLoop, calls=%fused_computation.90 | loop fusion | flops 25165824 | bytes 54525952 | tf_op jit(solution)/shard_map/mul | solution.py:252
  1103.8 8.8 fusion.41
  1112.5 9.8 slice.194
  1122.4 9.8 slice.195
  1135.5 9.4 copy.272
  1160.0 8.4 pad_maximum_fusion.4
  1168.5 8.9 copy.275
  1177.4 20.8 %add_bitcast_fusion.1 = (f32[1024,1024,1]{0,1,2:T(8,128)S(1)}, f32[1024,1024,1]{0,1,2:T(8,128)S(1)}) fusion(f32[1024,1024]{0,1:T(8,128)} %reshape.132, f32[1024,1024]{0,1:T(8,128)} %get-tuple-element.33, f32[1024,3]{0,1:T(4,128)S(1)} %get-tuple-element.58, f32[1024,3]{0,1:T(4,128)S(1)} %get-tuple-element.57), kind=kLoop, calls=%fused_computation.87 | loop fusion | flops 41943040 | bytes 16801792 | tf_op jit(solution)/shard_map/stack | solution.py:136
  1199.9 13.0 %copy.271 = f32[1024,1024,2]{0,2,1:T(2,128)} copy(f32[1024,1024,2]{0,1,2:T(8,128)S(1)} %pad_maximum_fusion.3) | data formatting | bytes 16777216 | tf_op jit(solution)/shard_map/stack | solution.py:136
  1212.8 11.0 reshape.133
  1224.7 7.5 multiply_bitcast_fusion
  1232.2 9.2 copy.265
  1241.4 13.6 %fusion.12 = f32[1024,2048]{0,1:T(8,128)} fusion(f32[1024,2048]{0,1:T(8,128)} %copy.272, f32[1024,2048]{0,1:T(8,128)} %reshape.133, f32[1024,8,256]{0,2,1:T(8,128)} %copy.265), kind=kLoop, calls=%fused_computation.33 | loop fusion | flops 8388608 | bytes 33554432 | tf_op jit(solution)/shard_map/max | solution.py:262
  1255.0 9.1 copy.273
  (137 shorter events, 109.0 us)
Async XLA Ops:
  7.2 625.7 %copy-start = (f32[128,128]{1,0:T(8,128)S(1)}, f32[128,128]{1,0:T(8,128)}, u32[]{:S(2)}) copy-start(f32[128,128]{1,0:T(8,128)} %param.15) | copy-start | bytes 196612
  7.2 21.8 %collective-permute-start = (s32[256]{0:T(256)}, s32[256]{0:T(256)S(1)}, u32[]{:S(2)}, u32[]{:S(2)}) collective-permute-start(s32[256]{0:T(256)} %param.16), channel_id=1, source_target_pairs={{0,31},{1,0},{2,1},{3,2},{4,3},{5,4},{6,5},{7,6},{8,7},{9,8},{10,9... | collective-permute-start | bytes 3080 | tf_op jit(solution)/shard_map/ppermute | solution.py:28
  22.9 6.1 copy-start.17
  22.9 146.8 %all-to-all-start = ((f32[1024,8,256]{0,2,1:T(8,128)}), f32[1024,8,256]{0,2,1:T(8,128)}, u32[]{:S(2)}, u32[]{:S(2)}) async-start(f32[1024,8,256]{0,2,1:T(8,128)} %bitcast.122), calls=%async_computation | async-start | bytes 16777216 | tf_op jit(solution)/shard_map/all_to_all | solution.py:181
  28.0 0.6 copy-start.15
  29.1 4.5 collective-permute-start.1
  33.6 85.5 %collective-permute-start.2 = (s32[1024]{0:T(1024)S(1)}, s32[1024]{0:T(1024)S(1)}, u32[]{:S(2)}, u32[]{:S(2)}) collective-permute-start(s32[1024]{0:T(1024)S(1)} %pad_add_fusion.1), channel_id=1, source_target_pairs={{0,28},{1,29},{2,30},{3,31},{4,0},{5,1},{6,2},{7,3},{8,4},{9,5},{1... | collective-permute-start | bytes 12296 | tf_op jit(solution)/shard_map/ppermute | solution.py:28
  119.1 3.9 collective-permute-start.3
  123.0 3.8 collective-permute-start.4
  124.7 71.8 %copy-start.8 = (f32[64,128]{0,1:T(8,128)}, f32[64,128]{0,1:T(8,128)S(1)}, u32[]{:S(2)}) copy-start(f32[64,128]{0,1:T(8,128)S(1)} %get-tuple-element.76) | copy-start | bytes 98308
  126.9 0.6 copy-start.10
  215.0 17.5 %slice-start.4 = ((s8[8388608]{0:T(1024)(128)(4,1)}), s8[4194304]{0:T(1024)(128)(4,1)S(1)}, s32[]{:S(2)}) async-start(s8[8388608]{0:T(1024)(128)(4,1)} %bitcast.127), calls=%async_computation.10 | async-start | bytes 8388608
  215.0 17.6 %slice-start.5 = ((s8[8388608]{0:T(1024)(128)(4,1)}), s8[4194304]{0:T(1024)(128)(4,1)S(1)}, s32[]{:S(2)}) async-start(s8[8388608]{0:T(1024)(128)(4,1)} %bitcast.127), calls=%async_computation.11 | async-start | bytes 8388608
  385.3 19.3 %copy-start.16 = (s32[256]{0:T(256)S(1)}, s32[256]{0:T(256)}, u32[]{:S(2)}) copy-start(s32[256]{0:T(256)} %copy-done.15) | copy-start | bytes 3076
  404.6 17.2 %copy-start.2 = (f32[8192,256]{0,1:T(8,128)S(1)}, f32[8192,256]{0,1:T(8,128)}, u32[]{:S(2)}) copy-start(f32[8192,256]{0,1:T(8,128)} %get-tuple-element.38) | copy-start | bytes 25165828
  421.9 29.4 %slice-start = ((s8[8388608]{0:T(1024)(128)(4,1)}), s8[4194304]{0:T(1024)(128)(4,1)S(1)}, s32[]{:S(2)}) async-start(s8[8388608]{0:T(1024)(128)(4,1)} %bitcast.120), calls=%async_computation.6 | async-start | bytes 8388608
  436.4 14.8 %slice-start.1 = ((s8[8388608]{0:T(1024)(128)(4,1)}), s8[4194304]{0:T(1024)(128)(4,1)S(1)}, s32[]{:S(2)}) async-start(s8[8388608]{0:T(1024)(128)(4,1)} %bitcast.120), calls=%async_computation.7 | async-start | bytes 8388608
  595.9 37.0 %copy-start.13 = (f32[256,2,128]{2,1,0:T(2,128)S(1)}, f32[256,2,128]{2,1,0:T(2,128)}, u32[]{:S(2)}) copy-start(f32[256,2,128]{2,1,0:T(2,128)} %param.14) | copy-start | bytes 786436
  595.9 37.0 %copy-start.14 = (f32[256,2,128]{2,1,0:T(2,128)S(1)}, f32[256,2,128]{2,1,0:T(2,128)}, u32[]{:S(2)}) copy-start(f32[256,2,128]{2,1,0:T(2,128)} %param.12) | copy-start | bytes 786436
  603.3 28.9 %all-to-all-start.2 = ((f32[1024,2,128]{2,1,0:T(2,128)}), f32[1024,2,128]{2,1,0:T(2,128)S(1)}, u32[]{:S(2)}, u32[]{:S(2)}) async-start(f32[1024,2,128]{2,1,0:T(2,128)} %reduce_sum.36), calls=%async_computation.2 | async-start | bytes 2097152 | tf_op jit(solution)/shard_map/all_to_all | solution.py:218
  606.9 97.1 %all-gather.3.cloned.1.call-start = ((), (), s32[]{:S(2)}) async-start(), calls=%async_computation.4 | async-start | bytes 1310720 | tf_op jit(solution)/shard_map/all_gather | solution.py:230
  672.8 0.7 copy-start.6
  674.6 136.5 %all-gather.5.cloned.1.call-start = ((), (), s32[]{:S(2)}) async-start(), calls=%async_computation.5 | async-start | bytes 9437184 | tf_op jit(solution)/shard_map/all_gather | solution.py:231
  704.0 11.3 slice-start.2
  705.0 10.4 slice-start.3
  705.0 10.4 collective-permute-start.5
  771.0 2.0 copy-start.5
  773.0 13.1 %collective-permute-start.6 = (f32[1024,6]{0,1:T(8,128)S(1)}, f32[1024,6]{0,1:T(8,128)S(1)}, u32[]{:S(2)}, u32[]{:S(2)}) collective-permute-start(f32[1024,6]{0,1:T(8,128)S(1)} %slice.235), channel_id=1, source_target_pairs={{1,0},{2,1},{3,2},{0,3},{5,4},{6,5},{7,6},{4,7},{9,8},{10,9},{11,1... | collective-permute-start | bytes 73736 | tf_op jit(solution)/shard_map/ppermute | solution.py:38
  780.8 5.4 copy-start.11
  811.1 10.0 copy-start.3
  992.0 13.2 %copy-start.9 = (f32[64,128]{0,1:T(8,128)S(1)}, f32[64,128]{0,1:T(8,128)}, u32[]{:S(2)}) copy-start(f32[64,128]{0,1:T(8,128)} %copy-done.8) | copy-start | bytes 98308
  992.0 13.2 %copy-start.12 = (f32[64,128]{0,1:T(8,128)S(1)}, f32[64,128]{0,1:T(8,128)}, u32[]{:S(2)}) copy-start(f32[64,128]{0,1:T(8,128)} %fusion.138) | copy-start | bytes 98308
  1026.7 16.3 %slice-start.6 = ((s8[8388608]{0:T(1024)(128)(4,1)}), s8[4194304]{0:T(1024)(128)(4,1)S(1)}, s32[]{:S(2)}) async-start(s8[8388608]{0:T(1024)(128)(4,1)} %bitcast.138), calls=%async_computation.12 | async-start | bytes 8388608
  1026.8 16.3 %slice-start.7 = ((s8[8388608]{0:T(1024)(128)(4,1)}), s8[4194304]{0:T(1024)(128)(4,1)S(1)}, s32[]{:S(2)}) async-start(s8[8388608]{0:T(1024)(128)(4,1)} %bitcast.138), calls=%async_computation.13 | async-start | bytes 8388608
  1063.3 5.1 copy-start.4
  1063.3 161.5 %all-to-all-start.3 = ((f32[8,1024,256]{2,1,0:T(8,128)}), f32[8,1024,256]{2,1,0:T(8,128)}, u32[]{:S(2)}, u32[]{:S(2)}) async-start(f32[8,1024,256]{2,1,0:T(8,128)} %bitcast.137), calls=%async_computation.3 | async-start | bytes 16777216 | tf_op jit(solution)/shard_map/all_to_all | solution.py:245
  1134.8 10.1 collective-permute-start.7
  1159.0 18.3 %collective-permute-start.8 = (f32[2,1024,3]{1,2,0:T(4,128)S(1)}, f32[2,1024,3]{1,2,0:T(4,128)S(1)}, u32[]{:S(2)}, u32[]{:S(2)}) collective-permute-start(f32[2,1024,3]{1,2,0:T(4,128)S(1)} %pad_maximum_fusion.11), channel_id=1, source_target_pairs={{3,0},{0,1},{1,2},{2,3},{7,4},{4,5},{5,6},{6,7},{11,8},{8,9},{9,10... | collective-permute-start | bytes 73736 | tf_op jit(solution)/shard_map/ppermute | solution.py:38
  1212.8 11.0 copy-start.7
  1241.4 22.8 %copy-start.1 = (f32[128,128]{1,0:T(8,128)S(1)}, f32[128,128]{1,0:T(8,128)}, u32[]{:S(2)}) copy-start(f32[128,128]{1,0:T(8,128)} %param.15) | copy-start | bytes 196612
Sparse Core Ops, SparseCore 0:
  674.7 29.2 all-gather.2
  705.9 53.6 all-gather.4
